TPU v7x, 256 devices: a whole 4x4x8 slice. The times are simulated.
256 devices in a mesh: seq: 32 (over z, y), tp: 8 (over x, core).
Axes of the slice: x: 4, y: 4, z: 8, core: 2. Of those that a mesh axis runs over, the one named last changes fastest.
Arguments:
- tokens: bfloat16 [384, 4096], P(None, 'seq'), may hold values from -30 to 30
- ln_first_gain: bfloat16 [4096], P('seq'), may hold values from 0.099609375 to 1.8984375
- w_qkv: bfloat16 [4096, 3, 4096], P('seq', None, 'tp'), may hold values from -0.25 to 0.25
- w_out: bfloat16 [4096, 4096], P('tp', 'seq'), may hold values from -1 to 1
- ln_second_gain: bfloat16 [4096], P('seq'), may hold values from 0.099609375 to 1.8984375
- w_up: bfloat16 [4096, 16384], P('seq', 'tp'), may hold values from -0.09375 to 0.09375
- w_down: bfloat16 [16384, 4096], P('tp', 'seq'), may hold values from -0.09375 to 0.09375
- prompt_key: bfloat16 [8, 16384, 4096], P(None, 'seq', 'tp'), may hold values from -200 to 200
- prompt_val: bfloat16 [8, 16384, 4096], P(None, 'seq', 'tp'), may hold values from -20 to 20
- cont_key: bfloat16 [96, 256, 4096], P('seq', None, 'tp'), may hold values from -18 to 18
- cont_val: bfloat16 [96, 256, 4096], P('seq', None, 'tp'), may hold values from -20 to 20
- group_ids: int32 [96], replicated, may hold values from 0 to 7, as said below
- prompt_len: int32 [8], replicated, may hold values from 1 to 16384, as said below
- cont_len: int32 [96], replicated, may hold values from 0 to 252, as said below
Outputs:
- layer_out: bfloat16 [384, 4096], P(None, 'seq')
Inputs may be any that keep to these rules, and one draw needn't show every extreme that they name: `group_ids`: each of the 8 groups is named by exactly 12 requests. `prompt_len`: one group's prompt has exactly 16384 positions. `cont_len`: some request has exactly 252 filled slots.
All inputs are finite; a program needn't handle non-finite values.
Results may differ from a plain program's by a relative error of at most 0.013.
The roundings to bfloat16 on the way count: a program that leaves them out, or rounds other values in their place, can miss the bound.
Values may be sent and summed in bfloat16 or wider, within the bound.
No kernel may reach another device: no remote copies, remote signals or barrier semaphores. Data moves between devices by JAX's collectives and lax.ppermute only.
A program may use at most 128 MiB of HBM per device.

v0:
```python
import math
import jax
import jax.numpy as jnp
from jax import lax
from jax.sharding import PartitionSpec as P

D = 4096
HEADS = 32
HD = 128
NEW = 4
NEG_FILL = -1e30
NORM_EPS = 1e-05


def finish_norm(values, row_sum, row_square, gain):
    mean_row = row_sum / D
    variance = row_square / D - mean_row * mean_row
    scaled = (values - mean_row[:, None]) * lax.rsqrt(variance + NORM_EPS)[:, None]
    return (scaled * gain.astype(jnp.float32)[None, :]).astype(jnp.bfloat16)


def combine_parts(earlier, later):
    merged_top = jnp.maximum(earlier[0], later[0])
    left_factor = jnp.exp(earlier[0] - merged_top)
    right_factor = jnp.exp(later[0] - merged_top)
    merged_sum = earlier[1] * left_factor + later[1] * right_factor
    merged_acc = earlier[2] * left_factor[..., None] + later[2] * right_factor[..., None]
    return (merged_top, merged_sum, merged_acc)


def body(
    tokens,
    ln_first_gain,
    w_qkv,
    w_out,
    ln_second_gain,
    w_up,
    w_down,
    prompt_key,
    prompt_val,
    cont_key,
    cont_val,
    group_ids,
    prompt_len,
    cont_len,
):
    row_count = tokens.shape[0]
    seq_index = lax.axis_index("seq")
    tp_index = lax.axis_index("tp")
    feat_width = w_qkv.shape[2]
    local_heads = feat_width // HD
    home_requests = cont_key.shape[0]
    home_rows = home_requests * NEW
    requests = row_count // NEW
    groups = prompt_key.shape[0]
    block_len = prompt_key.shape[1]
    slots = cont_key.shape[1]
    score_scale = 1.0 / math.sqrt(HD)
    token_float = tokens.astype(jnp.float32)
    first_sums = lax.psum((jnp.sum(token_float, 1), jnp.sum(token_float * token_float, 1)), "seq")
    normed = finish_norm(token_float, first_sums[0], first_sums[1], ln_first_gain)
    w_flat = w_qkv.reshape(w_qkv.shape[0], 3 * feat_width)
    partial_qkv = jnp.dot(normed, w_flat, preferred_element_type=jnp.float32)
    full_qkv = lax.psum(partial_qkv, "seq").astype(jnp.bfloat16)
    query = full_qkv[:, :feat_width]
    own_slice = lax.dynamic_slice_in_dim(full_qkv, seq_index * home_rows, home_rows, 0)
    key_new = own_slice[:, feat_width : 2 * feat_width]
    val_new = own_slice[:, 2 * feat_width :]
    head_first = (tp_index * local_heads).astype(jnp.float32)
    slopes = jnp.exp2(
        -8.0 * (head_first + jnp.arange(local_heads, dtype=jnp.float32) + 1.0) / HEADS
    )
    members = jnp.argsort(group_ids, stable=True).reshape(groups, requests // groups)
    inverse = jnp.argsort(members.reshape(-1))
    group_match = group_ids[:, None] == jnp.arange(groups, dtype=jnp.int32)[None, :]
    req_prompt = jnp.sum(jnp.where(group_match, prompt_len[None, :], 0), 1)
    query_pos = (req_prompt + cont_len)[:, None] + jnp.arange(NEW, dtype=jnp.int32)[None, :]
    query_req = query.reshape(requests, NEW, local_heads, HD)
    group_query = query_req[members].reshape(groups, -1, local_heads, HD)
    group_pos = query_pos[members].reshape(groups, -1)
    key_slab = prompt_key.reshape(groups, block_len, local_heads, HD)
    val_slab = prompt_val.reshape(groups, block_len, local_heads, HD)
    key_pos = seq_index * block_len + jnp.arange(block_len, dtype=jnp.int32)
    scores = jnp.einsum(
        "gqhd,gphd->ghqp", group_query, key_slab, preferred_element_type=jnp.float32
    )
    distance = (key_pos[None, None, :] - group_pos[:, :, None]).astype(jnp.float32)
    scores = scores * score_scale + slopes[None, :, None, None] * distance[:, None, :, :]
    is_live = (key_pos[None, :] < prompt_len[:, None])[:, None, None, :]
    block_top = jnp.max(jnp.where(is_live, scores, NEG_FILL), -1)
    weights = jnp.where(is_live, jnp.exp(scores - block_top[..., None]), 0.0)
    block_sum = jnp.sum(weights, -1)
    block_acc = jnp.einsum(
        "ghqp,gphd->gqhd",
        weights.astype(jnp.bfloat16),
        val_slab,
        preferred_element_type=jnp.float32,
    )
    prompt_top = (
        jnp.transpose(block_top, (0, 2, 1))
        .reshape(requests, NEW, local_heads)[inverse]
        .reshape(row_count, local_heads)
    )
    prompt_sum = (
        jnp.transpose(block_sum, (0, 2, 1))
        .reshape(requests, NEW, local_heads)[inverse]
        .reshape(row_count, local_heads)
    )
    prompt_acc = block_acc.reshape(requests, NEW, local_heads, HD)[inverse].reshape(
        row_count, local_heads, HD
    )
    home_query = lax.dynamic_slice_in_dim(query_req, seq_index * home_requests, home_requests, 0)
    home_pos = lax.dynamic_slice_in_dim(query_pos, seq_index * home_requests, home_requests, 0)
    home_prompt = lax.dynamic_slice_in_dim(req_prompt, seq_index * home_requests, home_requests, 0)
    home_filled = lax.dynamic_slice_in_dim(cont_len, seq_index * home_requests, home_requests, 0)
    cache_keys = cont_key.reshape(home_requests, slots, local_heads, HD)
    cache_vals = cont_val.reshape(home_requests, slots, local_heads, HD)
    slot_index = jnp.arange(slots, dtype=jnp.int32)
    cache_pos = home_prompt[:, None] + slot_index[None, :]
    cache_scores = (
        jnp.einsum("rjhd,rkhd->rhjk", home_query, cache_keys, preferred_element_type=jnp.float32)
        * score_scale
    )
    cache_scores = cache_scores + slopes[None, :, None, None] * (
        cache_pos[:, None, None, :] - home_pos[:, None, :, None]
    ).astype(jnp.float32)
    cache_live = (slot_index[None, :] < home_filled[:, None])[:, None, None, :]
    fresh_keys = key_new.reshape(home_requests, NEW, local_heads, HD)
    fresh_vals = val_new.reshape(home_requests, NEW, local_heads, HD)
    steps_new = jnp.arange(NEW, dtype=jnp.int32)
    fresh_dist = (steps_new[None, :] - steps_new[:, None]).astype(jnp.float32)
    fresh_scores = (
        jnp.einsum("rjhd,rkhd->rhjk", home_query, fresh_keys, preferred_element_type=jnp.float32)
        * score_scale
    )
    fresh_scores = fresh_scores + slopes[None, :, None, None] * fresh_dist[None, None, :, :]
    fresh_live = (steps_new[None, :] <= steps_new[:, None])[None, None, :, :]
    home_top = jnp.maximum(
        jnp.max(jnp.where(cache_live, cache_scores, NEG_FILL), -1),
        jnp.max(jnp.where(fresh_live, fresh_scores, NEG_FILL), -1),
    )
    cache_weights = jnp.where(cache_live, jnp.exp(cache_scores - home_top[..., None]), 0.0)
    fresh_weights = jnp.where(fresh_live, jnp.exp(fresh_scores - home_top[..., None]), 0.0)
    home_sum = jnp.sum(cache_weights, -1) + jnp.sum(fresh_weights, -1)
    home_acc = jnp.einsum(
        "rhjk,rkhd->rjhd",
        cache_weights.astype(jnp.bfloat16),
        cache_vals,
        preferred_element_type=jnp.float32,
    )
    home_acc = home_acc + jnp.einsum(
        "rhjk,rkhd->rjhd",
        fresh_weights.astype(jnp.bfloat16),
        fresh_vals,
        preferred_element_type=jnp.float32,
    )
    home_top = jnp.transpose(home_top, (0, 2, 1)).reshape(home_rows, local_heads)
    home_sum = jnp.transpose(home_sum, (0, 2, 1)).reshape(home_rows, local_heads)
    home_acc = home_acc.reshape(home_rows, local_heads, HD)
    row_start = seq_index * home_rows
    home_part = (
        lax.dynamic_update_slice_in_dim(
            jnp.full((row_count, local_heads), NEG_FILL, jnp.float32), home_top, row_start, 0
        ),
        lax.dynamic_update_slice_in_dim(
            jnp.zeros((row_count, local_heads), jnp.float32), home_sum, row_start, 0
        ),
        lax.dynamic_update_slice_in_dim(
            jnp.zeros((row_count, local_heads, HD), jnp.float32), home_acc, row_start, 0
        ),
    )
    local_part = combine_parts((prompt_top, prompt_sum, prompt_acc), home_part)
    global_top = lax.pmax(local_part[0], "seq")
    factor = jnp.exp(local_part[0] - global_top)
    merged_sum, merged_acc = lax.psum(
        (local_part[1] * factor, local_part[2] * factor[..., None]), "seq"
    )
    attended = (
        (merged_acc / merged_sum[..., None]).reshape(row_count, feat_width).astype(jnp.bfloat16)
    )
    attn_sum = lax.psum(jnp.dot(attended, w_out, preferred_element_type=jnp.float32), "tp")
    hidden_state = token_float + attn_sum
    second_sums = lax.psum(
        (jnp.sum(hidden_state, 1), jnp.sum(hidden_state * hidden_state, 1)), "seq"
    )
    second_normed = finish_norm(hidden_state, second_sums[0], second_sums[1], ln_second_gain)
    up_sum = lax.psum(jnp.dot(second_normed, w_up, preferred_element_type=jnp.float32), "seq")
    activated = jax.nn.gelu(up_sum, approximate=False).astype(jnp.bfloat16)
    down_part = jnp.dot(activated, w_down, preferred_element_type=jnp.float32)
    down_sum = lax.psum(down_part.astype(jnp.bfloat16), "tp").astype(jnp.float32)
    return (hidden_state + down_sum).astype(jnp.bfloat16)


def solution(mesh):
    in_specs = (
        P(None, "seq"),
        P("seq"),
        P("seq", None, "tp"),
        P("tp", "seq"),
        P("seq"),
        P("seq", "tp"),
        P("tp", "seq"),
        P(None, "seq", "tp"),
        P(None, "seq", "tp"),
        P("seq", None, "tp"),
        P("seq", None, "tp"),
        P(),
        P(),
        P(),
    )
    out_specs = P(None, "seq")
    return jax.shard_map(body, mesh=mesh, in_specs=in_specs, out_specs=out_specs, check_vma=False)
```

profile of v0, /device:TPU:8, one launch (start us, length us, event | category | flops | bytes accessed | tf_op | source)
XLA Modules:
  0.0 878.5 jit_solution(7815176637591646648)
XLA Ops:
  8.7 1.3 dynamic_slice.15
  9.9 1.2 convert_element_type.71
  11.2 3.2 sort.34
  16.3 1.2 gather_fusion.1
  17.5 1.2 copy.124
  18.7 73.8 %all-reduce.1 = (f32[384]{0:T(512)S(1)}, f32[384]{0:T(512)S(1)}) all-reduce(f32[384]{0:T(512)S(1)} %get-tuple-element.12, f32[384]{0:T(512)S(1)} %get-tuple-element.11), channel_id=1, replica_groups=mesh['seq'=32,'tp'=8] {'seq'}, use_global_device_ids=true, to_apply=%region_3.0 | all-reduce | flops 768 | bytes 6144 | tf_op jit(solution)/shard_map/psum | solution.py:60
  92.5 1.4 fusion.48
  93.9 165.3 %all-reduce.15 = bf16[384,1536]{1,0:T(8,128)(2,1)} all-reduce(f32[384,1536]{1,0:T(8,128)S(1)} %fusion.48), channel_id=1, replica_groups=mesh['seq'=32,'tp'=8] {'seq'}, use_global_device_ids=true, to_apply=%region_4.0 | all-reduce | flops 589824 | bytes 3538944 | tf_op jit(solution)/shard_map/psum | solution.py:64
  262.1 3.2 sort.35
  270.3 4.0 select_reduce_fusion
  275.4 1.5 fusion.27
  277.0 1.1 gather_fusion.2
  280.5 73.7 %pmax.7 = f32[384,4]{0,1:T(4,128)S(1)} all-reduce(f32[384,4]{0,1:T(4,128)S(1)} %max.18), channel_id=1, replica_groups=mesh['seq'=32,'tp'=8] {'seq'}, use_global_device_ids=true, to_apply=%region_11.12 | all-reduce | flops 1536 | bytes 12288 | tf_op jit(solution)/shard_map/pmax | solution.py:173
  354.8 1.5 add_multiply_fusion
  356.4 72.8 %psum.74 = f32[384,4]{0,1:T(4,128)S(1)} all-reduce(f32[384,4]{0,1:T(4,128)S(1)} %get-tuple-element.17), channel_id=1, replica_groups=mesh['seq'=32,'tp'=8] {'seq'}, use_global_device_ids=true, to_apply=%region_16.17 | all-reduce | flops 1536 | bytes 12288 | tf_op jit(solution)/shard_map/psum | solution.py:175
  429.3 72.5 %all-reduce.8.cloned.1.call-done = f32[384,4,128]{2,0,1:T(8,128)} async-done(((f32[384,4,128]{2,0,1:T(8,128)}), f32[384,4,128]{2,0,1:T(8,128)}) %all-reduce.8.cloned.1.call-update) | async-done | bytes 786448 | tf_op jit(solution)/shard_map/psum | solution.py:175
  501.8 1.4 divide_convert_fusion
  504.5 63.9 %all-reduce.10.cloned.1.call-done = f32[384,128]{1,0:T(8,128)} async-done(((f32[384,128]{1,0:T(8,128)}), f32[384,128]{1,0:T(8,128)}) %all-reduce.10.cloned.1.call-update) | async-done | bytes 196624 | tf_op jit(solution)/shard_map/psum | solution.py:181
  569.5 71.2 %all-reduce = (f32[384]{0:T(512)S(1)}, f32[384]{0:T(512)S(1)}) all-reduce(f32[384]{0:T(512)S(1)} %get-tuple-element.10, f32[384]{0:T(512)S(1)} %get-tuple-element.9), channel_id=1, replica_groups=mesh['seq'=32,'tp'=8] {'seq'}, use_global_device_ids=true, to_apply=%region_21.22 | all-reduce | flops 768 | bytes 6144 | tf_op jit(solution)/shard_map/psum | solution.py:183
  640.7 3.3 fusion.47
  644.3 154.8 %all-reduce.12.cloned.1.call-done = f32[384,2048]{1,0:T(8,128)} async-done(((f32[384,2048]{1,0:T(8,128)}), f32[384,2048]{1,0:T(8,128)}) %all-reduce.12.cloned.1.call-update) | async-done | bytes 3145744 | tf_op jit(solution)/shard_map/psum | solution.py:187
  799.1 9.0 %fusion.32 = bf16[384,128]{1,0:T(8,128)(2,1)} fusion(bf16[2048,128]{1,0:T(8,128)(2,1)S(1)} %copy-done.8, f32[384,2048]{1,0:T(8,128)} %all-reduce.12.cloned.1.call-done), kind=kOutput, calls=%fused_computation.43 | convolution fusion | flops 252493824 | bytes 3768320 | tf_op jit(solution)/shard_map/dot_general | solution.py:189
  808.2 62.2 %all-reduce.14.cloned.1.call-done = bf16[384,128]{1,0:T(8,128)(2,1)} async-done(((bf16[384,128]{1,0:T(8,128)(2,1)}), bf16[384,128]{1,0:T(8,128)(2,1)}) %all-reduce.14.cloned.1.call-update) | async-done | bytes 98320 | tf_op jit(solution)/shard_map/psum | solution.py:190
  870.4 1.6 add_convert_fusion
  (97 shorter events, 18.5 us)
Async XLA Ops:
  6.5 262.4 %copy-start = (bf16[3,256,512]{2,1,0:T(8,128)(2,1)S(1)}, bf16[3,256,512]{2,1,0:T(8,128)(2,1)}, u32[]{:S(2)}) copy-start(bf16[3,256,512]{2,1,0:T(8,128)(2,1)} %param.23) | copy-start | bytes 2359300
  6.5 495.3 %all-reduce.8.cloned.1.call-start = ((), (), s32[]{:S(2)}) async-start(), calls=%async_computation | async-start | bytes 1572864 | tf_op jit(solution)/shard_map/psum | solution.py:175
  14.4 0.5 copy-start.5
  259.2 10.4 %copy-start.7 = (bf16[3,256,512]{2,1,0:T(8,128)(2,1)S(1)}, bf16[3,256,512]{2,1,0:T(8,128)(2,1)}, u32[]{:S(2)}) copy-start(bf16[3,256,512]{2,1,0:T(8,128)(2,1)} %param.24) | copy-start | bytes 2359300
  270.3 5.1 copy-start.6
  280.1 223.3 %copy-start.4 = (bf16[512,128]{1,0:T(8,128)(2,1)S(1)}, bf16[512,128]{1,0:T(8,128)(2,1)}, u32[]{:S(2)}) copy-start(bf16[512,128]{1,0:T(8,128)(2,1)} %param.17) | copy-start | bytes 393220
  354.6 149.9 %copy-start.9 = (bf16[128]{0:T(256)(128)(2,1)S(1)}, bf16[128]{0:T(256)(128)(2,1)}, u32[]{:S(2)}) copy-start(bf16[128]{0:T(256)(128)(2,1)} %param.18) | copy-start | bytes 772
  354.6 213.8 %copy-start.1 = (bf16[384,128]{1,0:T(8,128)(2,1)S(1)}, bf16[384,128]{1,0:T(8,128)(2,1)}, u32[]{:S(2)}) copy-start(bf16[384,128]{1,0:T(8,128)(2,1)} %param.14) | copy-start | bytes 294916
  354.8 285.9 %copy-start.3 = (bf16[128,2048]{1,0:T(8,128)(2,1)S(1)}, bf16[128,2048]{1,0:T(8,128)(2,1)}, u32[]{:S(2)}) copy-start(bf16[128,2048]{1,0:T(8,128)(2,1)} %param.19) | copy-start | bytes 1572868
  356.4 212.0 %all-reduce.10.cloned.1.call-start = ((), (), s32[]{:S(2)}) async-start(), calls=%async_computation.1 | async-start | bytes 393216 | tf_op jit(solution)/shard_map/psum | solution.py:181
  504.4 294.6 %all-reduce.12.cloned.1.call-start = ((), (), s32[]{:S(2)}) async-start(), calls=%async_computation.2 | async-start | bytes 6291456 | tf_op jit(solution)/shard_map/psum | solution.py:187
  640.7 158.4 %copy-start.8 = (bf16[2048,128]{1,0:T(8,128)(2,1)S(1)}, bf16[2048,128]{1,0:T(8,128)(2,1)}, u32[]{:S(2)}) copy-start(bf16[2048,128]{1,0:T(8,128)(2,1)} %param.20) | copy-start | bytes 1572868
  644.1 226.3 %copy-start.2 = (f32[384,128]{1,0:T(8,128)S(1)}, f32[384,128]{1,0:T(8,128)}, u32[]{:S(2)}) copy-start(f32[384,128]{1,0:T(8,128)} %all-reduce.10.cloned.1.call-done) | copy-start | bytes 589828
  644.1 226.3 %all-reduce.14.cloned.1.call-start = ((), (), s32[]{:S(2)}) async-start(), calls=%async_computation.3 | async-start | bytes 196608 | tf_op jit(solution)/shard_map/psum | solution.py:190
Sparse Core Ops, SparseCore 0:
  356.5 145.2 all-reduce.7
  504.6 63.8 all-reduce.9
  644.2 154.8 all-reduce.11
  808.3 62.0 all-reduce.13
where the time goes:
time: 879 us; the launch traced here: 878 us
  blocking collectives  457 us (52%)
  waiting for transfers between devices  354 us (40%)
  matrix products  21.3 us (2%)
  other arithmetic  19.7 us (2%)
  between operations  13.5 us (2%)
  local copies, waits for them, and re-layouts  13.4 us (2%)
    psum x1, blocking collectives, body(): full_qkv = lax.psum(partial_qkv, 'seq').astype(jnp.bfloat16)  165 us
    psum x1, waiting for transfers between devices, body(): lax.psum(jnp.dot(second_normed, w_up, preferred_element_type=jnp.float32)...  155 us
    psum x1, blocking collectives, body(): lax.psum((jnp.sum(token_float, 1), jnp.sum(token_float * token_float, 1))...  73.8 us
    pmax x1, blocking collectives, body(): global_top = lax.pmax(local_part[0], 'seq')  73.7 us
    psum x1, blocking collectives, body(): lax.psum((local_part[1] * factor, local_part[2] * factor[..., None]), 'seq')  72.8 us
    psum x1, waiting for transfers between devices, body(): lax.psum((local_part[1] * factor, local_part[2] * factor[..., None]), 'seq')  72.5 us
    psum x1, blocking collectives, body(): lax.psum((jnp.sum(hidden_state, 1), jnp.sum(hidden_state * hidden_state,...  71.2 us
    psum x1, waiting for transfers between devices, body(): lax.psum(jnp.dot(attended, w_out, preferred_element_type=jnp.float32), 'tp')  63.9 us
  transfers between devices with their start and end apart: 4, of which 4 were waited for; matrix products, arithmetic and copies ran while one was open for 0% of the time, Pallas kernels for 0%

commit v1 on v0

--- a/solution.py
+++ b/solution.py
@@ -10,6 +10,10 @@
 NEW = 4
 NEG_FILL = -1e30
 NORM_EPS = 1e-05
+
+
+def shelves_refer(field):
+    return jnp.sum(lax.all_gather(field, "seq"), 0)
 
 
 def finish_norm(values, row_sum, row_square, gain):
@@ -61,7 +65,7 @@
     normed = finish_norm(token_float, first_sums[0], first_sums[1], ln_first_gain)
     w_flat = w_qkv.reshape(w_qkv.shape[0], 3 * feat_width)
     partial_qkv = jnp.dot(normed, w_flat, preferred_element_type=jnp.float32)
-    full_qkv = lax.psum(partial_qkv, "seq").astype(jnp.bfloat16)
+    full_qkv = shelves_refer(partial_qkv).astype(jnp.bfloat16)
     query = full_qkv[:, :feat_width]
     own_slice = lax.dynamic_slice_in_dim(full_qkv, seq_index * home_rows, home_rows, 0)
     key_new = own_slice[:, feat_width : 2 * feat_width]

time: 879 us -> 1210 us (1.38)
  waiting for transfers between devices: 354 us -> 825 us
  blocking collectives: 457 us -> 290 us
  other arithmetic: 19.7 us -> 43 us
    all_gather x0 -> x1, waiting for transfers between devices: none -> 469 us  [shelves_refer(): return jnp.sum(lax.all_gather(field, 'seq'), 0)]
    psum x1 -> x0, blocking collectives: 165 us -> none  [body(): full_qkv = lax.psum(partial_qkv, 'seq').astype(jnp.bfloat16)]
    reduce_sum x0 -> x1, other arithmetic: none -> 23.7 us  [shelves_refer(): return jnp.sum(lax.all_gather(field, 'seq'), 0)]
  transfers between devices with their start and end apart: 4 -> 5, of which waited for: 4 -> 5; matrix products, arithmetic and copies ran while one was open for 0% -> 1% of each run, Pallas kernels for 0% -> 0%
where the time goes in v1:
time: 1210 us
  waiting for transfers between devices  825 us (68%)
  blocking collectives  290 us (24%)
  other arithmetic  43 us (4%)
  matrix products  28.6 us (2%)
  between operations  13.5 us (1%)
    all_gather x1, waiting for transfers between devices, shelves_refer(): return jnp.sum(lax.all_gather(field, 'seq'), 0)  469 us
    psum x1, waiting for transfers between devices, body(): lax.psum(jnp.dot(second_normed, w_up, preferred_element_type=jnp.float32)...  155 us
    psum x1, waiting for transfers between devices, body(): lax.psum((local_part[1] * factor, local_part[2] * factor[..., None]), 'seq')  74.7 us
    psum x1, blocking collectives, body(): lax.psum((jnp.sum(token_float, 1), jnp.sum(token_float * token_float, 1))...  73.8 us
    psum x1, blocking collectives, body(): lax.psum((local_part[1] * factor, local_part[2] * factor[..., None]), 'seq')  72.6 us
    pmax x1, blocking collectives, body(): global_top = lax.pmax(local_part[0], 'seq')  72.3 us
    psum x1, blocking collectives, body(): lax.psum((jnp.sum(hidden_state, 1), jnp.sum(hidden_state * hidden_state,...  71.2 us
    psum x1, waiting for transfers between devices, body(): lax.psum(jnp.dot(attended, w_out, preferred_element_type=jnp.float32), 'tp')  63.9 us
  transfers between devices with their start and end apart: 5, of which 5 were waited for; matrix products, arithmetic and copies ran while one was open for 1% of the time, Pallas kernels for 0%

profile of v1, /device:TPU:8, one launch (start us, length us, event | category | flops | bytes accessed | tf_op | source)
XLA Modules:
  0.0 1209.1 jit_solution(10604268702318646172)
XLA Ops:
  6.6 1.1 convert_reduce_fusion
  7.7 1.2 copy.122
  9.6 73.8 %all-reduce.1 = (f32[384]{0:T(512)S(1)}, f32[384]{0:T(512)S(1)}) all-reduce(f32[384]{0:T(512)S(1)} %get-tuple-element.12, f32[384]{0:T(512)S(1)} %get-tuple-element.11), channel_id=1, replica_groups=mesh['seq'=32,'tp'=8] {'seq'}, use_global_device_ids=true, to_apply=%region_3.0 | all-reduce | flops 768 | bytes 6144 | tf_op jit(solution)/shard_map/psum | solution.py:64
  83.4 2.9 fusion.48
  86.6 2.5 sort.34
  90.1 2.5 sort.35
  96.1 469.0 %all-gather.3.cloned.1.call-done = f32[12288,1536]{1,0:T(8,128)} async-done(((f32[384,1536]{1,0:T(8,128)}), f32[12288,1536]{1,0:T(8,128)}) %all-gather.3.cloned.1.call-update) | async-done | bytes 75497488 | tf_op jit(solution)/shard_map/all_gather | solution.py:16
  565.1 23.7 %reduce_sum.83 = bf16[384,1536]{1,0:T(8,128)(2,1)S(1)} reduce(f32[32,384,1536]{2,1,0:T(8,128)} %bitcast.1, f32[]{:T(128)} %constant.49.clone.1), dimensions={0}, to_apply=%region_4.0 | reduce | flops 18284544 | bytes 76677120 | tf_op jit(solution)/shard_map/reduce_sum | solution.py:16
  592.8 5.4 select_reduce_fusion
  599.7 72.3 %pmax.7 = f32[384,4]{0,1:T(4,128)S(1)} all-reduce(f32[384,4]{0,1:T(4,128)S(1)} %max.18), channel_id=1, replica_groups=mesh['seq'=32,'tp'=8] {'seq'}, use_global_device_ids=true, to_apply=%region_11.12 | all-reduce | flops 1536 | bytes 12288 | tf_op jit(solution)/shard_map/pmax | solution.py:177
  672.4 3.0 fusion.16
  676.9 4.4 fusion.27
  681.4 1.3 gather_fusion.2
  683.5 1.5 add_multiply_fusion
  685.1 72.6 %psum.66 = f32[384,4]{0,1:T(4,128)S(1)} all-reduce(f32[384,4]{0,1:T(4,128)S(1)} %get-tuple-element.17), channel_id=1, replica_groups=mesh['seq'=32,'tp'=8] {'seq'}, use_global_device_ids=true, to_apply=%region_16.17 | all-reduce | flops 1536 | bytes 12288 | tf_op jit(solution)/shard_map/psum | solution.py:179
  757.6 74.7 %all-reduce.7.cloned.1.call-done = f32[384,4,128]{2,0,1:T(8,128)} async-done(((f32[384,4,128]{2,0,1:T(8,128)}), f32[384,4,128]{2,0,1:T(8,128)}) %all-reduce.7.cloned.1.call-update) | async-done | bytes 786448 | tf_op jit(solution)/shard_map/psum | solution.py:179
  832.3 1.4 divide_convert_fusion
  835.1 63.9 %all-reduce.9.cloned.1.call-done = f32[384,128]{1,0:T(8,128)} async-done(((f32[384,128]{1,0:T(8,128)}), f32[384,128]{1,0:T(8,128)}) %all-reduce.9.cloned.1.call-update) | async-done | bytes 196624 | tf_op jit(solution)/shard_map/psum | solution.py:185
  900.1 71.2 %all-reduce = (f32[384]{0:T(512)S(1)}, f32[384]{0:T(512)S(1)}) all-reduce(f32[384]{0:T(512)S(1)} %get-tuple-element.10, f32[384]{0:T(512)S(1)} %get-tuple-element.9), channel_id=1, replica_groups=mesh['seq'=32,'tp'=8] {'seq'}, use_global_device_ids=true, to_apply=%region_21.22 | all-reduce | flops 768 | bytes 6144 | tf_op jit(solution)/shard_map/psum | solution.py:187
  971.2 3.3 fusion.47
  974.8 154.9 %all-reduce.11.cloned.1.call-done = f32[384,2048]{1,0:T(8,128)} async-done(((f32[384,2048]{1,0:T(8,128)}), f32[384,2048]{1,0:T(8,128)}) %all-reduce.11.cloned.1.call-update) | async-done | bytes 3145744 | tf_op jit(solution)/shard_map/psum | solution.py:191
  1129.7 9.0 fusion.32
  1138.7 62.2 %all-reduce.13.cloned.1.call-done = bf16[384,128]{1,0:T(8,128)(2,1)} async-done(((bf16[384,128]{1,0:T(8,128)(2,1)}), bf16[384,128]{1,0:T(8,128)(2,1)}) %all-reduce.13.cloned.1.call-update) | async-done | bytes 98320 | tf_op jit(solution)/shard_map/psum | solution.py:194
  1201.0 1.6 add_convert_fusion
  (110 shorter events, 16.1 us)
Async XLA Ops:
  6.5 584.1 %copy-start = (bf16[3,256,512]{2,1,0:T(8,128)(2,1)S(1)}, bf16[3,256,512]{2,1,0:T(8,128)(2,1)}, u32[]{:S(2)}) copy-start(bf16[3,256,512]{2,1,0:T(8,128)(2,1)} %param.23) | copy-start | bytes 2359300
  6.5 79.8 %copy-start.13 = (s32[96]{0:T(128)S(1)}, s32[96]{0:T(128)}, u32[]{:S(2)}) copy-start(s32[96]{0:T(128)} %param.25) | copy-start | bytes 1156
  6.5 79.8 %copy-start.9 = (s32[8]{0:T(128)S(1)}, s32[8]{0:T(128)}, u32[]{:S(2)}) copy-start(s32[8]{0:T(128)} %param.26) | copy-start | bytes 100
  6.5 79.9 %copy-start.12 = (s32[96]{0:T(128)S(1)}, s32[96]{0:T(128)}, u32[]{:S(2)}) copy-start(s32[96]{0:T(128)} %param.27) | copy-start | bytes 1156
  6.5 558.6 %all-gather.3.cloned.1.call-start = ((), (), s32[]{:S(2)}) async-start(), calls=%async_computation.4 | async-start | bytes 77856768 | tf_op jit(solution)/shard_map/all_gather | solution.py:16
  86.2 746.1 %all-reduce.7.cloned.1.call-start = ((), (), s32[]{:S(2)}) async-start(), calls=%async_computation | async-start | bytes 1572864 | tf_op jit(solution)/shard_map/psum | solution.py:179
  93.2 2.1 copy-start.5
  592.7 79.3 %copy-start.8 = (pred[4,4]{0,1:T(4,128)(4,1)S(1)}, pred[4,4]{0,1:T(4,128)(4,1)}, u32[]{:S(2)}) copy-start(pred[4,4]{0,1:T(4,128)(4,1)} %iota_compare_fusion.2) | copy-start | bytes 52
  592.7 79.3 %copy-start.7 = (pred[3,256]{1,0:T(4,128)(4,1)S(1)}, pred[3,256]{1,0:T(4,128)(4,1)}, u32[]{:S(2)}) copy-start(pred[3,256]{1,0:T(4,128)(4,1)} %iota_compare_fusion) | copy-start | bytes 2308
  592.7 79.6 %copy-start.6 = (f32[4]{0:T(128)S(1)}, f32[4]{0:T(128)}, u32[]{:S(2)}) copy-start(f32[4]{0:T(128)} %copy-done.5) | copy-start | bytes 52
  598.2 78.2 %copy-start.10 = (bf16[3,256,512]{2,1,0:T(8,128)(2,1)S(1)}, bf16[3,256,512]{2,1,0:T(8,128)(2,1)}, u32[]{:S(2)}) copy-start(bf16[3,256,512]{2,1,0:T(8,128)(2,1)} %param.24) | copy-start | bytes 2359300
  682.9 151.1 %copy-start.4 = (bf16[512,128]{1,0:T(8,128)(2,1)S(1)}, bf16[512,128]{1,0:T(8,128)(2,1)}, u32[]{:S(2)}) copy-start(bf16[512,128]{1,0:T(8,128)(2,1)} %param.17) | copy-start | bytes 393220
  683.2 151.8 %copy-start.14 = (bf16[128]{0:T(256)(128)(2,1)S(1)}, bf16[128]{0:T(256)(128)(2,1)}, u32[]{:S(2)}) copy-start(bf16[128]{0:T(256)(128)(2,1)} %param.18) | copy-start | bytes 772
  683.2 215.7 %copy-start.1 = (bf16[384,128]{1,0:T(8,128)(2,1)S(1)}, bf16[384,128]{1,0:T(8,128)(2,1)}, u32[]{:S(2)}) copy-start(bf16[384,128]{1,0:T(8,128)(2,1)} %param.14) | copy-start | bytes 294916
  683.5 287.8 %copy-start.3 = (bf16[128,2048]{1,0:T(8,128)(2,1)S(1)}, bf16[128,2048]{1,0:T(8,128)(2,1)}, u32[]{:S(2)}) copy-start(bf16[128,2048]{1,0:T(8,128)(2,1)} %param.19) | copy-start | bytes 1572868
  685.0 213.9 %all-reduce.9.cloned.1.call-start = ((), (), s32[]{:S(2)}) async-start(), calls=%async_computation.1 | async-start | bytes 393216 | tf_op jit(solution)/shard_map/psum | solution.py:185
  835.0 294.7 %all-reduce.11.cloned.1.call-start = ((), (), s32[]{:S(2)}) async-start(), calls=%async_computation.2 | async-start | bytes 6291456 | tf_op jit(solution)/shard_map/psum | solution.py:191
  971.2 158.4 %copy-start.11 = (bf16[2048,128]{1,0:T(8,128)(2,1)S(1)}, bf16[2048,128]{1,0:T(8,128)(2,1)}, u32[]{:S(2)}) copy-start(bf16[2048,128]{1,0:T(8,128)(2,1)} %param.20) | copy-start | bytes 1572868
  974.6 226.4 %copy-start.2 = (f32[384,128]{1,0:T(8,128)S(1)}, f32[384,128]{1,0:T(8,128)}, u32[]{:S(2)}) copy-start(f32[384,128]{1,0:T(8,128)} %all-reduce.9.cloned.1.call-done) | copy-start | bytes 589828
  974.6 226.4 %all-reduce.13.cloned.1.call-start = ((), (), s32[]{:S(2)}) async-start(), calls=%async_computation.3 | async-start | bytes 196608 | tf_op jit(solution)/shard_map/psum | solution.py:194
Sparse Core Ops, SparseCore 0:
  86.4 478.6 all-gather.2
  685.1 147.1 all-reduce.6
  835.1 63.8 all-reduce.8
  974.7 154.9 all-reduce.10
  1138.9 62.0 all-reduce.12
